TPU v7x, 32 devices: a whole 2x2x4 slice. The times are simulated.
32 devices in a mesh: row: 8 (over z, x), col: 4 (over y, core).
Axes of the slice: x: 2, y: 2, z: 4, core: 2. Of those that a mesh axis runs over, the one named last changes fastest.
Arguments:
- amplitudes: bfloat16 [3072, 65536], P('row', 'col'), may hold values from -6 to 6
- integrals: bfloat16 [65536, 1024], P('col', 'row'), may hold values from -0.09375 to 0.09375
- pair_label: int32 [24], P('row'), may hold values from 0 to 7
- orbital_irrep: int32 [256], replicated, may hold values from 0 to 7
- column_label: int32 [8], replicated, may hold values from 0 to 7
Outputs:
- ladder: bfloat16 [1024, 3072], P('col', 'row')
Inputs may be any that keep to these rules, and one draw needn't show every extreme that they name: `orbital_irrep`: irrep labels of the window's virtual orbitals.
All inputs are finite; a program needn't handle non-finite values.
Results may differ from a plain program's by a relative error of at most 0.001.
Values may be sent and summed in bfloat16 or wider, within the bound.
No kernel may reach another device: no remote copies, remote signals or barrier semaphores. Data moves between devices by JAX's collectives and lax.ppermute only.
A program may use at most 128 MiB of HBM per device.

v0:
```python
import jax
import jax.numpy as jnp
from jax import lax
from jax.experimental import pallas as pl
from jax.experimental.pallas import tpu as pltpu
from jax.sharding import PartitionSpec as P

PAIR_BLOCK = 128
IRREPS = 8
TIERS = (4, 5, 6, 8)


def _compact_kernel(base_ref, pos_ref, src_ref, out_ref, acc_ref, *, lists, width, sub, subs, steps):
    b = pl.program_id(0)
    span = sub + 16

    @pl.when(b == 0)
    def _():
        acc_ref[...] = jnp.zeros_like(acc_ref)

    rows = lax.broadcasted_iota(jnp.int32, (span, sub), 0)
    for l in range(lists):
        for k in range(subs):
            start = pl.multiple_of(base_ref[(l * steps + b) * subs + k], 16)
            onehot = (rows == pos_ref[l:l + 1, k * sub:(k + 1) * sub] - start).astype(src_ref.dtype)
            part = jnp.dot(
                onehot, src_ref[k * sub:(k + 1) * sub, l * width:(l + 1) * width], preferred_element_type=jnp.float32
            )
            acc_ref[pl.ds(start, span), l * width:(l + 1) * width] += part

    @pl.when(b == steps - 1)
    def _():
        out_ref[...] = acc_ref[: out_ref.shape[0], :].astype(out_ref.dtype)


def compact_rows(source, masks, chunk, cap, lists, width):
    total, _ = source.shape
    chunks = total // chunk
    sub = min(128, chunk)
    step = min(2048, chunk)
    steps = total // step
    flat = masks.reshape(lists, chunks, chunk).astype(jnp.int32)
    rank = jnp.cumsum(flat, axis=2) - flat
    offset = jnp.arange(chunks, dtype=jnp.int32)[None, :, None] * cap
    pos = jnp.where((flat > 0) & (rank < cap), offset + rank, -1).reshape(lists, total)
    first = (offset + jnp.minimum(rank, cap)).reshape(lists, total // sub, sub)[:, :, 0]
    base = ((first // 16) * 16).reshape(lists * (total // sub))
    kept = chunks * cap
    return pl.pallas_call(
        lambda *refs: _compact_kernel(*refs, lists=lists, width=width, sub=sub, subs=step // sub, steps=steps),
        out_shape=jax.ShapeDtypeStruct((kept, lists * width), source.dtype),
        grid_spec=pltpu.PrefetchScalarGridSpec(
            num_scalar_prefetch=1,
            grid=(steps,),
            in_specs=[
                pl.BlockSpec((lists, step), lambda b, base: (0, b)),
                pl.BlockSpec((step, lists * width), lambda b, base: (b, 0)),
            ],
            out_specs=pl.BlockSpec((kept, lists * width), lambda b, base: (0, 0)),
            scratch_shapes=[pltpu.VMEM((kept + sub + 16, lists * width), jnp.float32)],
        ),
        compiler_params=pltpu.CompilerParams(dimension_semantics=("arbitrary",)),
    )(base, pos, source)


def make_body(n_row, n_col):
    def body(amplitudes, integrals, pair_label, orbital_irrep, column_label):
        pair_rows, cd_count = amplitudes.shape
        orb_width = orbital_irrep.shape[0]
        c_count = cd_count // orb_width
        ab_count = integrals.shape[1]
        col_i = lax.axis_index("col")
        row_i = lax.axis_index("row")
        c_irrep = lax.dynamic_slice_in_dim(orbital_irrep, col_i * c_count, c_count)
        cd_label = jnp.bitwise_xor(c_irrep[:, None], orbital_irrep[None, :]).reshape(cd_count)
        row_label = jnp.repeat(pair_label, pair_rows // pair_label.shape[0])

        def dense(_):
            int_cube = integrals.reshape(c_count, orb_width, ab_count)
            swapped = lax.all_to_all(int_cube, "col", split_axis=1, concat_axis=0, tiled=True)
            mirrored = jnp.transpose(swapped, (1, 0, 2)).reshape(cd_count, ab_count)
            ab_label = jnp.repeat(column_label, PAIR_BLOCK)
            amp_keep = row_label[:, None] == cd_label[None, :]
            slab_keep = cd_label[:, None] == ab_label[None, :]
            amp_kept = jnp.where(amp_keep, amplitudes, jnp.zeros_like(amplitudes))
            int_slab = lax.all_gather(integrals, "row", axis=1, tiled=True)
            mirror_slab = lax.all_gather(mirrored, "row", axis=1, tiled=True)
            int_kept = jnp.where(slab_keep, int_slab, jnp.zeros_like(int_slab))
            mirror_kept = jnp.where(slab_keep, mirror_slab, jnp.zeros_like(mirror_slab))
            direct = jnp.einsum("ka,pk->ap", int_kept, amp_kept, preferred_element_type=jnp.float32)
            crossed = jnp.einsum("ka,pk->ap", mirror_kept, amp_kept, preferred_element_type=jnp.float32)
            return direct - crossed

        single = ab_count <= PAIR_BLOCK and PAIR_BLOCK % ab_count == 0
        if not single:
            partial = dense(None)
        else:
            block_label = column_label[(jnp.arange(n_row) * ab_count) // PAIR_BLOCK]
            irreps = jnp.arange(IRREPS, dtype=orbital_irrep.dtype)
            blk_irrep = orbital_irrep.reshape(n_col, c_count)
            blk_cnt = jnp.sum(blk_irrep[:, :, None] == irreps[None, None, :], axis=1)
            xor_tab = jnp.bitwise_xor(irreps[:, None], irreps[None, :])
            pair_cnt = jnp.einsum("ak,bkl->abl", blk_cnt, blk_cnt[:, xor_tab])
            largest = jnp.max(pair_cnt[:, :, block_label])
            pair_cells = c_count * c_count
            caps = [t * pair_cells // 16 for t in TIERS]
            tier = sum((largest > cap).astype(jnp.int32) for cap in caps)
            own_irrep = blk_irrep[col_i]
            n_pb = pair_label.shape[0]
            pb = pair_rows // n_pb

            lab_jdc = jnp.bitwise_xor(blk_irrep[:, :, None], own_irrep[None, None, :])
            lab_bcd = jnp.bitwise_xor(own_irrep[None, :, None], blk_irrep[:, None, :])
            p_lab = pair_label.astype(lab_jdc.dtype)

            def compact(cap):
                def run(_):
                    int_jdc = jnp.transpose(integrals.reshape(c_count, n_col, c_count, ab_count), (1, 2, 0, 3))
                    int_jdc = int_jdc.reshape(cd_count, ab_count)
                    sent = compact_rows(
                        int_jdc, (lab_jdc == block_label[row_i])[None], pair_cells, cap, 1, ab_count
                    )
                    got = lax.all_gather(sent, "row", axis=0, tiled=False)
                    amp_jcd = jnp.transpose(amplitudes.reshape(pair_rows, c_count, n_col, c_count), (2, 1, 3, 0))
                    amp_jcd = amp_jcd.reshape(cd_count, pair_rows)
                    amp_dc = jnp.transpose(amplitudes.reshape(pair_rows, c_count, orb_width), (2, 1, 0))
                    amp_dc = amp_dc.reshape(cd_count, pair_rows)
                    outgoing = compact_rows(
                        amp_jcd, lab_bcd[None] == p_lab[:, None, None, None], pair_cells, cap, n_pb, pb
                    )
                    incoming = lax.all_to_all(outgoing, "col", split_axis=0, concat_axis=0, tiled=True)
                    direct = compact_rows(
                        amp_dc, lab_jdc[None] == p_lab[:, None, None, None], pair_cells, cap, n_pb, pb
                    )
                    both = jnp.concatenate([direct, incoming], axis=1)
                    prod = jnp.einsum("imq,mx->iqx", got, both, preferred_element_type=jnp.float32)
                    diff = prod[..., :pair_rows] - prod[..., pair_rows:]
                    keep = block_label[:, None] == row_label[None, :]
                    diff = jnp.where(keep[:, None, :], diff, jnp.zeros_like(diff))
                    return diff.reshape(n_row * ab_count, pair_rows)

                return run

            branches = [compact(cap) for cap in caps] + [dense]
            partial = lax.switch(tier, branches, None)
        summed = lax.psum_scatter(partial, "col", scatter_dimension=0, tiled=True)
        return summed.astype(jnp.bfloat16)

    return body


def solution(mesh):
    placed = (P("row", "col"), P("col", "row"), P("row"), P(), P())
    return jax.shard_map(
        make_body(mesh.shape["row"], mesh.shape["col"]),
        mesh=mesh,
        in_specs=placed,
        out_specs=P("col", "row"),
        check_vma=False,
    )
```

profile of v0, /device:TPU:0, one launch (start us, length us, event | category | flops | bytes accessed | tf_op | source)
XLA Modules:
  0.0 257.0 jit_solution(1115542208269290500)
XLA Ops:
  7.4 0.8 eq.403
  8.2 0.1 convert_reduce_fusion
  8.3 0.1 copy.284
  8.4 0.1 reshape.1503
  8.5 0.6 gather_fusion
  9.1 0.2 fusion.115
  9.3 1.3 gather_fusion.1
  10.6 0.6 gather_fusion.2
  11.2 0.6 reduce_max.9
  14.4 0.7 broadcast_in_dim.87
  15.2 202.8 %conditional.1 = (f32[1024,384]{1,0:T(8,128)S(1)}) conditional(s32[]{:T(128)} %clamp.3, (s32[8]{0:T(128)S(1)}, s32[3,128]{1,0:T(4,128)S(1)}, s32[]{:T(128)}, s32[4,64]{1,0:T(4,128)S(1)}, bf16[16384,128]{1,0:T(8,128)(2,1)}, /*index=5*/s32[3]{0:T(128)}, bf16[384,16384]{1,0:T(8,128)(2,1)}, s32[64]{0:T(128)S(1)}, ...), branch_computations={%region_2.9_spmd, %region_9.16_spmd, %region_16.23_spmd, %region_2... | conditional | flops 25862488064 | bytes 357389376 | solution.py:145
  22.5 0.6 dynamic_slice.13
  23.1 0.7 compare_convert_fusion.5
  23.9 0.1 reshape.1492
  23.9 0.1 reshape.1494
  24.1 0.1 reshape.1493
  24.2 1.2 reduce-window.56
  25.3 0.2 slice_reduce_fusion.5
  25.6 0.2 reduce-window.57
  25.8 0.1 broadcast_bitcast_fusion.4
  25.9 0.1 reshape.1432
  26.0 0.1 add.384
  26.1 0.2 fusion.51
  26.3 0.5 fusion.61.refs_0_
  26.8 6.8 %copy.268 = bf16[64,4,64,128]{3,0,2,1:T(8,128)(2,1)} copy(bf16[64,4,64,128]{3,2,1,0:T(8,128)(2,1)} %bitcast.380) | data formatting | bytes 8388608 | tf_op jit(solution)/shard_map/cond/branch_1_fun/reshape | solution.py:118
  33.7 0.8 and_select_fusion.2.refs_1_
  34.5 8.8 %branch_1_fun.3 = bf16[5120,128]{1,0:T(8,128)(2,1)} custom-call(s32[128]{0:T(128)} %fusion.61.refs_0_, s32[1,16384]{1,0:T(1,128)} %and_select_fusion.2.refs_1_, bf16[16384,128]{1,0:T(8,128)(2,1)} %bitcast.404), custom_call_target="tpu_custom_call" | custom-call | tf_op jit(solution)/shard_map/cond/branch_1_fun/pallas_call | solution.py:49
  43.3 0.1 broadcast_xor_fusion.2
  43.4 0.1 eq.315
  43.5 0.1 eq.323
  43.6 0.1 eq.327
  43.7 0.1 eq.333
  43.8 0.1 eq.319
  43.8 0.1 eq.330
  43.9 0.1 compare_convert_fusion.3
  44.0 3.5 %reduce-window.60 = s32[3,4,32,128]{3,2,1,0:T(8,128)S(1)} reduce-window(s32[3,4,32,128]{3,2,1,0:T(8,128)S(1)} %get-tuple-element.468, s32[]{:T(128)} %constant.199.clone), window={size=1x1x1x128 pad=0_0x0_0x0_0x127_0}, to_apply=%region_12.12 | reduce-window | flops 6242304 | bytes 393220 | tf_op jit(solution)/shard_map/reduce-window.8
  47.5 0.4 slice_reduce_fusion.4
  47.9 0.6 reduce-window.61
  48.5 3.5 %reduce-window.62 = s32[3,4,32,128]{3,2,1,0:T(8,128)S(1)} reduce-window(s32[3,4,32,128]{3,2,1,0:T(8,128)S(1)} %get-tuple-element.467, s32[]{:T(128)} %constant.199.clone), window={size=1x1x1x128 pad=0_0x0_0x0_0x127_0}, to_apply=%region_14.14 | reduce-window | flops 6242304 | bytes 393220 | tf_op jit(solution)/shard_map/reduce-window.10
  52.0 0.4 slice_reduce_fusion.3
  52.4 0.6 reduce-window.65
  53.0 0.1 broadcast_bitcast_fusion.3
  53.1 0.1 reshape.1440
  53.2 0.1 reshape.1445
  53.3 0.1 add.392
  53.4 15.8 %copy.288 = bf16[384,16384]{0,1:T(8,128)(2,1)} copy(bf16[384,16384]{1,0:T(8,128)(2,1)} %get-tuple-element.423) | data formatting | bytes 25165824 | tf_op jit(solution)/shard_map
  69.2 10.8 %copy.270 = bf16[4,64,64,384]{3,2,1,0:T(8,128)(2,1)} copy(bf16[4,64,64,384]{3,2,0,1:T(8,128)(2,1)} %bitcast.386) | data formatting | bytes 25165824 | tf_op jit(solution)/shard_map/cond/branch_1_fun/transpose | solution.py:124
  80.0 0.3 fusion.50
  80.3 0.6 fusion.56.refs_0_
  80.9 0.1 broadcast_add_fusion.3
  81.1 0.1 broadcast_add_fusion.2
  81.2 1.2 add_select_fusion.5
  82.4 14.9 %branch_1_fun.5 = bf16[5120,384]{1,0:T(8,128)(2,1)} custom-call(s32[384]{0:T(512)} %fusion.56.refs_0_, s32[3,16384]{1,0:T(4,128)} %get-tuple-element.464.refs_1_, bf16[16384,384]{1,0:T(8,128)(2,1)} %bitcast.393), custom_call_target="tpu_custom_call" | custom-call | tf_op jit(solution)/shard_map/cond/branch_1_fun/pallas_call | solution.py:49
  97.4 5.4 %all-to-all-start.1 = ((bf16[4,1280,384]{2,1,0:T(8,128)(2,1)}), bf16[4,1280,384]{2,1,0:T(8,128)(2,1)}, u32[]{:S(2)}, u32[]{:S(2)}) async-start(bf16[4,1280,384]{2,1,0:T(8,128)(2,1)} %bitcast.409), calls=%async_computation.1 | async-start | bytes 7864320 | tf_op jit(solution)/shard_map/cond/branch_1_fun/all_to_all | solution.py:131
  102.7 14.9 %copy.269 = bf16[384,64,256]{0,1,2:T(8,128)(2,1)} copy(bf16[384,64,256]{0,2,1:T(8,128)(2,1)} %bitcast.387) | data formatting | bytes 25165824 | tf_op jit(solution)/shard_map/cond/branch_1_fun/reshape | solution.py:126
  117.6 0.6 fusion.54.refs_0_
  118.2 14.9 %branch_1_fun.4 = bf16[5120,384]{1,0:T(8,128)(2,1)} custom-call(s32[384]{0:T(512)} %fusion.54.refs_0_, s32[3,16384]{1,0:T(4,128)} %get-tuple-element.463.refs_1_, bf16[16384,384]{1,0:T(8,128)(2,1)} %bitcast.397), custom_call_target="tpu_custom_call" | custom-call | tf_op jit(solution)/shard_map/cond/branch_1_fun/pallas_call | solution.py:49
  133.2 16.2 %all-to-all-done.1 = bf16[4,1280,384]{2,1,0:T(8,128)(2,1)} async-done(((bf16[4,1280,384]{2,1,0:T(8,128)(2,1)}), bf16[4,1280,384]{2,1,0:T(8,128)(2,1)}, u32[]{:S(2)}, u32[]{:S(2)}) %all-to-all-start.1) | async-done | bytes 3932192 | tf_op jit(solution)/shard_map/cond/branch_1_fun/all_to_all | solution.py:131
  149.4 47.6 %all-gather.13.cloned.1.call-done = bf16[40960,128]{1,0:T(8,128)(2,1)} async-done(((bf16[5120,128]{1,0:T(8,128)(2,1)}), bf16[40960,128]{1,0:T(8,128)(2,1)}) %all-gather.13.cloned.1.call-update) | async-done | bytes 10485776 | tf_op jit(solution)/shard_map/cond/branch_1_fun/all_gather | solution.py:123
  197.0 12.8 %fusion.37 = f32[8,128,768]{2,1,0:T(8,128)S(1)} fusion(bf16[8,5120,128]{2,1,0:T(8,128)(2,1)} %bitcast.491, bf16[5120,384]{1,0:T(8,128)(2,1)} %bitcast.41, bf16[5120,384]{1,0:T(8,128)(2,1)} %branch_1_fun.4), kind=kOutput, calls=%fused_computation.91 | convolution fusion | flops 8068792320 | bytes 21495808 | tf_op jit(solution)/shard_map/cond/branch_1_fun/imq,mx->iqx/dot_general | solution.py:136
  209.8 0.2 fusion.40
  218.1 1.1 copy-done.1
  219.2 28.2 %reduce-scatter.2.cloned.1.call-done = f32[256,384]{1,0:T(8,128)} async-done(((f32[1024,384]{1,0:T(8,128)}), f32[256,384]{1,0:T(8,128)}) %reduce-scatter.2.cloned.1.call-update) | async-done | bytes 393232 | tf_op jit(solution)/shard_map/reduce_scatter | solution.py:146
  247.3 1.7 convert_element_type.267
  (22 shorter events, 0.5 us)
Async XLA Ops:
  22.5 174.5 %all-gather.13.cloned.1.call-start = ((), (), s32[]{:S(2)}) async-start(), calls=%async_computation.7 | async-start | bytes 11796480 | tf_op jit(solution)/shard_map/cond/branch_1_fun/all_gather | solution.py:123
  33.6 10.3 %copy-start.3 = (s32[3]{0:T(128)S(1)}, s32[3]{0:T(128)}, u32[]{:S(2)}) copy-start(s32[3]{0:T(128)} %get-tuple-element.98) | copy-start | bytes 40 | tf_op jit(solution)/shard_map/cond
  97.4 52.0 %all-to-all-start.1 = ((bf16[4,1280,384]{2,1,0:T(8,128)(2,1)}), bf16[4,1280,384]{2,1,0:T(8,128)(2,1)}, u32[]{:S(2)}, u32[]{:S(2)}) async-start(bf16[4,1280,384]{2,1,0:T(8,128)(2,1)} %bitcast.409), calls=%async_computation.1 | async-start | bytes 7864320 | tf_op jit(solution)/shard_map/cond/branch_1_fun/all_to_all | solution.py:131
  218.0 1.2 copy-start.1
  218.0 29.3 %reduce-scatter.2.cloned.1.call-start = ((), (), s32[]{:S(2)}) async-start(), calls=%async_computation.12 | async-start | bytes 1966080 | tf_op jit(solution)/shard_map/reduce_scatter | solution.py:146
Sparse Core Ops, SparseCore 0:
  43.4 153.5 all-gather.12
Sparse Core Ops, SparseCore 1:
  221.0 26.3 reduce-scatter.1
where the time goes:
time: 254 us; the launch traced here: 257 us
  waiting for transfers between devices  92 us (36%)
  local copies, waits for them, and re-layouts  56.7 us (22%)
  Pallas kernels  38.6 us (15%)
  between operations  18 us (7%)
  other arithmetic  17.8 us (7%)
  loops' own time  15.5 us (6%)
  matrix products  13 us (5%)
  starting transfers between devices  5.46 us (2%)
    all_gather x1, waiting for transfers between devices, run(): got = lax.all_gather(sent, 'row', axis=0, tiled=False)  47.6 us
    pallas_call x3, Pallas kernels, compact_rows(): pl.pallas_call(lambda *refs: _compact_kernel(*refs, lists=lists, width=wi...  38.6 us
    reduce_scatter x1, waiting for transfers between devices, body(): summed = lax.psum_scatter(partial, 'col', scatter_dimension=0, tiled=True)  28.2 us
    another operation x9, local copies, waits for them, and re-layouts  17.1 us
    all_to_all x1, waiting for transfers between devices, run(): lax.all_to_all(outgoing, 'col', split_axis=0, concat_axis=0, tiled=True)  16.2 us
    another operation x1, loops' own time, body(): partial = lax.switch(tier, branches, None)  15.5 us
    reshape x1, local copies, waits for them, and re-layouts, run(): amplitudes.reshape(pair_rows, c_count, orb_width)  14.9 us
    dot_general x1, matrix products, run(): jnp.einsum('imq,mx->iqx', got, both, preferred_element_type=jnp.float32)  12.8 us
  transfers between devices with their start and end apart: 3, of which 3 were waited for; matrix products, arithmetic and copies ran while one was open for 21% of the time, Pallas kernels for 12%

commit v1 on v0

--- a/solution.py
+++ b/solution.py
@@ -63,6 +63,41 @@
     )(base, pos, source)
 
 
+def _ladder_kernel(match_ref, got_ref, both_ref, out_ref, *, n_pb, pb):
+    i = pl.program_id(0)
+    half = n_pb * pb
+    for u in range(n_pb):
+
+        @pl.when(match_ref[i * n_pb + u] != 0)
+        def _():
+            g = got_ref[0]
+            direct = jnp.dot(g, both_ref[:, u * pb:(u + 1) * pb], preferred_element_type=jnp.float32)
+            crossed = jnp.dot(g, both_ref[:, half + u * pb:half + (u + 1) * pb], preferred_element_type=jnp.float32)
+            out_ref[0, :, u * pb:(u + 1) * pb] = direct - crossed
+
+        @pl.when(match_ref[i * n_pb + u] == 0)
+        def _():
+            out_ref[0, :, u * pb:(u + 1) * pb] = jnp.zeros((out_ref.shape[1], pb), out_ref.dtype)
+
+
+def ladder_blocks(match, got_t, both, n_pb, pb):
+    n_blk, ab, rows = got_t.shape
+    return pl.pallas_call(
+        lambda *refs: _ladder_kernel(*refs, n_pb=n_pb, pb=pb),
+        out_shape=jax.ShapeDtypeStruct((n_blk, ab, n_pb * pb), jnp.float32),
+        grid_spec=pltpu.PrefetchScalarGridSpec(
+            num_scalar_prefetch=1,
+            grid=(n_blk,),
+            in_specs=[
+                pl.BlockSpec((1, ab, rows), lambda i, m: (i, 0, 0)),
+                pl.BlockSpec((rows, 2 * n_pb * pb), lambda i, m: (0, 0)),
+            ],
+            out_specs=pl.BlockSpec((1, ab, n_pb * pb), lambda i, m: (i, 0, 0)),
+        ),
+        compiler_params=pltpu.CompilerParams(dimension_semantics=("arbitrary",), vmem_limit_bytes=60 * 1024 * 1024),
+    )(match, got_t, both)
+
+
 def make_body(n_row, n_col):
     def body(amplitudes, integrals, pair_label, orbital_irrep, column_label):
         pair_rows, cd_count = amplitudes.shape
@@ -120,7 +155,7 @@
                     sent = compact_rows(
                         int_jdc, (lab_jdc == block_label[row_i])[None], pair_cells, cap, 1, ab_count
                     )
-                    got = lax.all_gather(sent, "row", axis=0, tiled=False)
+                    got = lax.all_gather(sent.T, "row", axis=0, tiled=False)
                     amp_jcd = jnp.transpose(amplitudes.reshape(pair_rows, c_count, n_col, c_count), (2, 1, 3, 0))
                     amp_jcd = amp_jcd.reshape(cd_count, pair_rows)
                     amp_dc = jnp.transpose(amplitudes.reshape(pair_rows, c_count, orb_width), (2, 1, 0))
@@ -133,18 +168,18 @@
                         amp_dc, lab_jdc[None] == p_lab[:, None, None, None], pair_cells, cap, n_pb, pb
                     )
                     both = jnp.concatenate([direct, incoming], axis=1)
-                    prod = jnp.einsum("imq,mx->iqx", got, both, preferred_element_type=jnp.float32)
-                    diff = prod[..., :pair_rows] - prod[..., pair_rows:]
-                    keep = block_label[:, None] == row_label[None, :]
-                    diff = jnp.where(keep[:, None, :], diff, jnp.zeros_like(diff))
+                    match = (block_label[:, None] == pair_label[None, :]).astype(jnp.int32).reshape(n_row * n_pb)
+                    diff = ladder_blocks(match, got, both, n_pb, pb)
                     return diff.reshape(n_row * ab_count, pair_rows)
 
                 return run
 
             branches = [compact(cap) for cap in caps] + [dense]
             partial = lax.switch(tier, branches, None)
-        summed = lax.psum_scatter(partial, "col", scatter_dimension=0, tiled=True)
-        return summed.astype(jnp.bfloat16)
+        parts = lax.all_to_all(
+            partial.reshape(n_col, partial.shape[0] // n_col, pair_rows), "col", split_axis=0, concat_axis=0, tiled=True
+        )
+        return jnp.sum(parts, axis=0).astype(jnp.bfloat16)
 
     return body
 

time: 254 us -> 255 us (level)
  waiting for transfers between devices: 92 us -> 55.4 us
  blocking collectives: 0 us -> 22.6 us
  local copies, waits for them, and re-layouts: 56.7 us -> 70.2 us
  matrix products: 13 us -> 0.18 us
  Pallas kernels: 38.6 us -> 49.1 us
  other arithmetic: 17.8 us -> 23.8 us
    reduce_scatter x1 -> x0, waiting for transfers between devices: 28.2 us -> none  [body(): summed = lax.psum_scatter(partial, 'col', scatter_dimension=0, tiled=True)]
    all_to_all x0 -> x1, blocking collectives: none -> 22.6 us  [body(): lax.all_to_all(partial.reshape(n_col, partial.shape[0] // n_col, pair_row...]
    all_gather x0 -> x1, local copies, waits for them, and re-layouts: none -> 13.7 us  [run(): got = lax.all_gather(sent.T, 'row', axis=0, tiled=False)]
    dot_general x1 -> x0, matrix products: 12.8 us -> none  [run(): jnp.einsum('imq,mx->iqx', got, both, preferred_element_type=jnp.float32)]
    pallas_call x0 -> x1, Pallas kernels: none -> 10.5 us  [ladder_blocks(): pl.pallas_call(lambda *refs: _ladder_kernel(*refs, n_pb=n_pb, pb=pb), out...]
    all_gather x1, waiting for transfers between devices: 47.6 us -> 40.4 us  [run(): got = lax.all_gather(sent.T, 'row', axis=0, tiled=False)]
    concatenate x0 -> x1, other arithmetic: none -> 7.08 us  [run(): both = jnp.concatenate([direct, incoming], axis=1)]
  transfers between devices with their start and end apart: 3 -> 2, of which waited for: 3 -> 2; matrix products, arithmetic and copies ran while one was open for 21% -> 25% of each run, Pallas kernels for 12% -> 12%
where the time goes in v1:
time: 255 us; the launch traced here: 257 us
  local copies, waits for them, and re-layouts  70.2 us (28%)
  waiting for transfers between devices  55.4 us (22%)
  Pallas kernels  49.1 us (19%)
  other arithmetic  23.8 us (9%)
  blocking collectives  22.6 us (9%)
  between operations  16.3 us (6%)
  loops' own time  14 us (5%)
  starting transfers between devices  5.31 us (2%)
    all_gather x1, waiting for transfers between devices, run(): got = lax.all_gather(sent.T, 'row', axis=0, tiled=False)  40.4 us
    pallas_call x3, Pallas kernels, compact_rows(): pl.pallas_call(lambda *refs: _compact_kernel(*refs, lists=lists, width=wi...  38.6 us
    all_to_all x1, blocking collectives, body(): lax.all_to_all(partial.reshape(n_col, partial.shape[0] // n_col, pair_row...  22.6 us
    another operation x9, local copies, waits for them, and re-layouts  18.1 us
    all_to_all x1, waiting for transfers between devices, run(): lax.all_to_all(outgoing, 'col', split_axis=0, concat_axis=0, tiled=True)  15 us
    reshape x1, local copies, waits for them, and re-layouts, run(): amplitudes.reshape(pair_rows, c_count, orb_width)  14.7 us
    another operation x1, loops' own time, body(): partial = lax.switch(tier, branches, None)  14 us
    all_gather x1, local copies, waits for them, and re-layouts, run(): got = lax.all_gather(sent.T, 'row', axis=0, tiled=False)  13.7 us
  transfers between devices with their start and end apart: 2, of which 2 were waited for; matrix products, arithmetic and copies ran while one was open for 25% of the time, Pallas kernels for 12%

profile of v1, /device:TPU:0, one launch (start us, length us, event | category | flops | bytes accessed | tf_op | source)
XLA Modules:
  0.0 256.9 jit_solution(5340674959861351915)
XLA Ops:
  6.6 0.8 eq.387
  7.3 0.1 convert_reduce_fusion
  7.5 0.1 copy.284
  7.5 0.1 reshape.1439
  7.6 0.6 gather_fusion
  8.2 0.2 fusion.95
  8.4 1.3 gather_fusion.1
  9.8 0.6 gather_fusion.2
  10.3 0.6 reduce_max.9
  13.6 212.7 %conditional.1 = (f32[1024,384]{1,0:T(8,128)S(1)}) conditional(s32[]{:T(128)} %clamp.3, (s32[8]{0:T(128)S(1)}, s32[3]{0:T(128)}, s32[]{:T(128)}, s32[4,64]{1,0:T(4,128)S(1)}, bf16[16384,128]{1,0:T(8,128)(2,1)}, /*index=5*/bf16[384,16384]{1,0:T(8,128)(2,1)}, s32[64]{0:T(128)S(1)}, s32[64]{0:T(128)S(1)}, ...), branch_computations={%region_2.9_spmd, %region_9.16_spmd, %region_16.23_spmd, %region_2... | conditional | flops 25862488064 | bytes 357391040 | solution.py:178
  20.7 0.6 dynamic_slice.13
  21.3 0.7 compare_convert_fusion.6
  22.0 0.1 reshape.1426
  22.1 0.1 reshape.1428
  22.2 0.1 reshape.1427
  22.3 1.2 reduce-window.56
  23.5 0.2 slice_reduce_fusion.5
  23.7 0.2 reduce-window.57
  23.9 0.1 broadcast_bitcast_fusion.5
  24.1 0.1 reshape.1362
  24.2 0.1 add.382
  24.3 0.2 fusion.42
  24.5 0.5 fusion.52.refs_0_
  25.0 6.8 %copy.268 = bf16[64,4,64,128]{3,0,2,1:T(8,128)(2,1)} copy(bf16[64,4,64,128]{3,2,1,0:T(8,128)(2,1)} %bitcast.366) | data formatting | bytes 8388608 | tf_op jit(solution)/shard_map/cond/branch_1_fun/reshape | solution.py:153
  31.9 0.8 and_select_fusion.2.refs_1_
  32.7 8.8 %branch_1_fun.4 = bf16[5120,128]{1,0:T(8,128)(2,1)} custom-call(s32[128]{0:T(128)} %fusion.52.refs_0_, s32[1,16384]{1,0:T(1,128)} %and_select_fusion.2.refs_1_, bf16[16384,128]{1,0:T(8,128)(2,1)} %bitcast.394), custom_call_target="tpu_custom_call" | custom-call | tf_op jit(solution)/shard_map/cond/branch_1_fun/pallas_call | solution.py:49
  41.4 0.1 broadcast_xor_fusion.2
  41.5 0.1 eq.301
  41.6 0.1 eq.309
  41.7 0.1 eq.313
  41.8 0.1 eq.319
  41.9 0.1 eq.305
  42.0 0.1 eq.316
  42.1 0.1 compare_convert_fusion.4
  42.2 3.5 %reduce-window.60 = s32[3,4,32,128]{3,2,1,0:T(8,128)S(1)} reduce-window(s32[3,4,32,128]{3,2,1,0:T(8,128)S(1)} %get-tuple-element.429, s32[]{:T(128)} %constant.195.clone), window={size=1x1x1x128 pad=0_0x0_0x0_0x127_0}, to_apply=%region_12.12 | reduce-window | flops 6242304 | bytes 393220 | tf_op jit(solution)/shard_map/reduce-window.8
  45.7 0.4 slice_reduce_fusion.4
  46.1 0.6 reduce-window.61
  46.7 3.5 %reduce-window.62 = s32[3,4,32,128]{3,2,1,0:T(8,128)S(1)} reduce-window(s32[3,4,32,128]{3,2,1,0:T(8,128)S(1)} %get-tuple-element.428, s32[]{:T(128)} %constant.195.clone), window={size=1x1x1x128 pad=0_0x0_0x0_0x127_0}, to_apply=%region_14.14 | reduce-window | flops 6242304 | bytes 393220 | tf_op jit(solution)/shard_map/reduce-window.10
  50.1 0.4 slice_reduce_fusion.3
  50.5 0.6 reduce-window.65
  51.2 0.1 broadcast_bitcast_fusion.4
  51.2 0.1 reshape.1370
  51.3 0.1 reshape.1375
  51.5 0.1 add.390
  51.6 16.8 %copy.288 = bf16[384,16384]{0,1:T(8,128)(2,1)} copy(bf16[384,16384]{1,0:T(8,128)(2,1)} %get-tuple-element.386) | data formatting | bytes 25165824 | tf_op jit(solution)/shard_map
  68.4 10.8 %copy.271 = bf16[4,64,64,384]{3,2,1,0:T(8,128)(2,1)} copy(bf16[4,64,64,384]{3,2,0,1:T(8,128)(2,1)} %bitcast.372) | data formatting | bytes 25165824 | tf_op jit(solution)/shard_map/cond/branch_1_fun/transpose | solution.py:159
  79.1 0.3 fusion.41
  79.5 0.6 fusion.47.refs_0_
  80.1 0.1 broadcast_add_fusion.3
  80.2 0.1 broadcast_add_fusion.2
  80.3 1.2 add_select_fusion.5
  81.6 14.9 %branch_1_fun.6 = bf16[5120,384]{1,0:T(8,128)(2,1)} custom-call(s32[384]{0:T(512)} %fusion.47.refs_0_, s32[3,16384]{1,0:T(4,128)} %get-tuple-element.425.refs_1_, bf16[16384,384]{1,0:T(8,128)(2,1)} %bitcast.380), custom_call_target="tpu_custom_call" | custom-call | tf_op jit(solution)/shard_map/cond/branch_1_fun/pallas_call | solution.py:49
  96.5 5.3 %all-to-all-start.1 = ((bf16[4,1280,384]{2,1,0:T(8,128)(2,1)}), bf16[4,1280,384]{2,1,0:T(8,128)(2,1)}, u32[]{:S(2)}, u32[]{:S(2)}) async-start(bf16[4,1280,384]{2,1,0:T(8,128)(2,1)} %bitcast.399), calls=%async_computation.1 | async-start | bytes 7864320 | tf_op jit(solution)/shard_map/cond/branch_1_fun/all_to_all | solution.py:166
  101.8 14.7 %copy.270 = bf16[384,64,256]{0,1,2:T(8,128)(2,1)} copy(bf16[384,64,256]{0,2,1:T(8,128)(2,1)} %bitcast.373) | data formatting | bytes 25165824 | tf_op jit(solution)/shard_map/cond/branch_1_fun/reshape | solution.py:161
  116.6 0.7 reshape.1425.refs_0_
  117.3 0.6 fusion.45.refs_0_
  117.8 14.9 %branch_1_fun.5 = bf16[5120,384]{1,0:T(8,128)(2,1)} custom-call(s32[384]{0:T(512)} %fusion.45.refs_0_, s32[3,16384]{1,0:T(4,128)} %get-tuple-element.424.refs_1_, bf16[16384,384]{1,0:T(8,128)(2,1)} %bitcast.384), custom_call_target="tpu_custom_call" | custom-call | tf_op jit(solution)/shard_map/cond/branch_1_fun/pallas_call | solution.py:49
  132.8 15.0 %all-to-all-done.1 = bf16[4,1280,384]{2,1,0:T(8,128)(2,1)} async-done(((bf16[4,1280,384]{2,1,0:T(8,128)(2,1)}), bf16[4,1280,384]{2,1,0:T(8,128)(2,1)}, u32[]{:S(2)}, u32[]{:S(2)}) %all-to-all-start.1) | async-done | bytes 3932192 | tf_op jit(solution)/shard_map/cond/branch_1_fun/all_to_all | solution.py:166
  147.7 7.1 %pad_maximum_fusion.1.refs_2_ = bf16[5120,768]{1,0:T(8,128)(2,1)} fusion(bf16[5120,384]{1,0:T(8,128)(2,1)} %bitcast.40, bf16[5120,384]{1,0:T(8,128)(2,1)} %branch_1_fun.5), kind=kLoop, calls=%fused_computation.85 | loop fusion | flops 15728640 | bytes 15728640 | tf_op jit(solution)/shard_map/cond/branch_1_fun/concatenate | solution.py:170
  154.8 40.4 %all-gather.13.cloned.1.call-done = bf16[1024,5120]{0,1:T(8,128)(2,1)} async-done(((bf16[128,5120]{0,1:T(8,128)(2,1)}), bf16[1024,5120]{0,1:T(8,128)(2,1)}) %all-gather.13.cloned.1.call-update) | async-done | bytes 10485776 | tf_op jit(solution)/shard_map/cond/branch_1_fun/all_gather | solution.py:158
  195.2 13.7 %copy.269 = bf16[1024,5120]{1,0:T(8,128)(2,1)} copy(bf16[1024,5120]{0,1:T(8,128)(2,1)} %all-gather.13.cloned.1.call-done) | data formatting | bytes 20971520 | tf_op jit(solution)/shard_map/cond/branch_1_fun/all_gather | solution.py:158
  209.0 10.5 %branch_1_fun.7 = f32[8,128,384]{2,1,0:T(8,128)S(1)} custom-call(s32[24]{0:T(128)} %reshape.1425.refs_0_, bf16[8,128,5120]{2,1,0:T(8,128)(2,1)} %bitcast.388, bf16[5120,768]{1,0:T(8,128)(2,1)} %pad_maximum_fusion.1.refs_2_), custom_call_target="tpu_custom_call" | custom-call | tf_op jit(solution)/shard_map/cond/branch_1_fun/pallas_call | solution.py:85
  226.3 22.6 %all_to_all.56 = f32[4,256,384]{2,1,0:T(8,128)S(1)} all-to-all(f32[4,256,384]{2,1,0:T(8,128)S(1)} %bitcast.407), channel_id=1, replica_groups=mesh['row'=8,'col'=4] {'col'}, dimensions={0} | all-to-all | bytes 3145728 | tf_op jit(solution)/shard_map/all_to_all | solution.py:179
  249.0 0.8 reduce_sum.19
  (19 shorter events, 0.5 us)
Async XLA Ops:
  20.6 21.5 %copy-start.2 = (s32[3]{0:T(128)S(1)}, s32[3]{0:T(128)}, u32[]{:S(2)}) copy-start(s32[3]{0:T(128)} %get-tuple-element.85) | copy-start | bytes 40 | tf_op jit(solution)/shard_map/cond
  20.6 174.6 %all-gather.13.cloned.1.call-start = ((), (), s32[]{:S(2)}) async-start(), calls=%async_computation.7 | async-start | bytes 11796480 | tf_op jit(solution)/shard_map/cond/branch_1_fun/all_gather | solution.py:158
  96.5 51.3 %all-to-all-start.1 = ((bf16[4,1280,384]{2,1,0:T(8,128)(2,1)}), bf16[4,1280,384]{2,1,0:T(8,128)(2,1)}, u32[]{:S(2)}, u32[]{:S(2)}) async-start(bf16[4,1280,384]{2,1,0:T(8,128)(2,1)} %bitcast.399), calls=%async_computation.1 | async-start | bytes 7864320 | tf_op jit(solution)/shard_map/cond/branch_1_fun/all_to_all | solution.py:166
Sparse Core Ops, SparseCore 0:
  41.6 153.6 all-gather.12
